TPU v7x, 256 devices: a whole 4x4x8 slice. The times are simulated.
256 devices in a mesh: tm: 32 (over x_lo, z, core), cell: 8 (over y, x_hi).
Axes of the slice: x: 4 (x_hi: 2, x_lo: 2; x = x_hi * 2 + x_lo), y: 4, z: 8, core: 2. Of those that a mesh axis runs over, the one named last changes fastest.
Arguments:
- velocity: bfloat16 [4096, 512, 96], P('cell', 'tm'), may hold values from -6 to 6
- cell_coords: int32 [4096, 3], P('cell'), may hold values from 0 to 15, as said below
- q_coords: int32 [512, 3], replicated, may hold values from 0 to 15
- eigvecs: float32 [512, 2, 96, 96], P(('tm', 'cell')), may hold values from -0.4375 to 0.4375
Outputs:
- power: float32 [512, 96, 512], P(('tm', 'cell'))
Inputs may be any that keep to these rules, and one draw needn't show every extreme that they name: `cell_coords`: every row names a distinct lattice position, each coordinate in 0 to 15.
All inputs are finite; a program needn't handle non-finite values.
Results may differ from a plain program's by a relative error of at most 0.015.
Values may be sent and summed in bfloat16 or wider, within the bound.
No kernel may reach another device: no remote copies, remote signals or barrier semaphores. Data moves between devices by JAX's collectives and lax.ppermute only.
A program may use at most 64 MiB of HBM per device.

v0:
```python
import math
import jax
import jax.numpy as jnp
from jax import lax
from jax.sharding import PartitionSpec as P

L = 16


def phase_rows(q_coords, cell_coords):
    products = (
        q_coords[:, None, 0] * cell_coords[None, :, 0]
        + q_coords[:, None, 1] * cell_coords[None, :, 1]
        + q_coords[:, None, 2] * cell_coords[None, :, 2]
    )
    step = jnp.arange(4, dtype=jnp.float32) * (2.0 * math.pi / L)
    cos_table = jnp.cos(step).astype(jnp.bfloat16)
    sin_table = (-jnp.sin(step)).astype(jnp.bfloat16)
    bit0 = products & 1 != 0
    bit1 = products & 2 != 0
    bit2 = products & 4 != 0
    bit3 = products & 8 != 0
    real = jnp.where(
        bit1,
        jnp.where(bit0, cos_table[3], cos_table[2]),
        jnp.where(bit0, cos_table[1], cos_table[0]),
    )
    imag = jnp.where(
        bit1,
        jnp.where(bit0, sin_table[3], sin_table[2]),
        jnp.where(bit0, sin_table[1], sin_table[0]),
    )
    real, imag = (jnp.where(bit2, imag, real), jnp.where(bit2, -real, imag))
    real, imag = (jnp.where(bit3, -real, real), jnp.where(bit3, -imag, imag))
    return jnp.stack([real, imag], axis=1)


def twiddles(frames):
    inner = 16
    outer = frames // inner
    w = jnp.arange(frames, dtype=jnp.int32)
    a = jnp.arange(outer, dtype=jnp.int32)
    b = jnp.arange(inner, dtype=jnp.int32)
    coarse = (a[:, None] * w[None, :] % outer).astype(jnp.float32) * (2.0 * math.pi / outer)
    fine = (b[:, None] * w[None, :] % frames).astype(jnp.float32) * (2.0 * math.pi / frames)
    cos_c, sin_c = (jnp.cos(coarse)[:, None, :], jnp.sin(coarse)[:, None, :])
    cos_f, sin_f = (jnp.cos(fine)[None, :, :], jnp.sin(fine)[None, :, :])
    cosines = (cos_c * cos_f - sin_c * sin_f).reshape(frames, frames)
    sines = (sin_c * cos_f + cos_c * sin_f).reshape(frames, frames)
    return (cosines, sines)


def local(velocity, cell_coords, q_coords, eigvecs):
    n_tm = lax.axis_size("tm")
    n_cell = lax.axis_size("cell")
    n_dev = n_tm * n_cell
    cell_dev, frames_dev, branches = velocity.shape
    q_total = q_coords.shape[0]
    q_local = q_total // n_dev
    frames = frames_dev * n_tm
    frames_each = frames_dev // n_cell
    spread = velocity.reshape(cell_dev, n_cell, frames_each * branches)
    all_cells = lax.all_to_all(spread, "cell", split_axis=1, concat_axis=0, tiled=True)
    all_cells = all_cells.reshape(cell_dev * n_cell, frames_each * branches)
    all_coords = lax.all_gather(cell_coords, "cell", axis=0, tiled=True)
    table = phase_rows(q_coords, all_coords).reshape(2 * q_total, cell_dev * n_cell)
    modes = jnp.dot(table, all_cells, preferred_element_type=jnp.float32)
    modes = modes.astype(jnp.bfloat16).reshape(n_dev, q_local, 2, frames_each, branches)
    collected = lax.all_to_all(modes, ("tm", "cell"), split_axis=0, concat_axis=0, tiled=True)
    scale = 1.0 / math.sqrt(cell_dev * n_cell)
    e_real = eigvecs[:, 0] * scale
    e_imag = eigvecs[:, 1] * scale
    e_block = jnp.stack(
        [jnp.concatenate([e_real, -e_imag], axis=2), jnp.concatenate([e_imag, e_real], axis=2)],
        axis=1,
    )
    highest = lax.Precision.HIGHEST
    amplitude = jnp.einsum(
        "sjrfk,jrkc->jsfc", collected.astype(jnp.float32), e_block, precision=highest
    ).reshape(q_local, frames, 2 * branches)
    cosines, sines = twiddles(frames)
    basis = jnp.concatenate([cosines, sines], axis=1)
    projected = jnp.einsum("jts,tw->jsw", amplitude, basis, precision=highest)
    on_cos = projected[:, :, :frames]
    on_sin = projected[:, :, frames:]
    out_real = on_cos[:, :branches] + on_sin[:, branches:]
    out_imag = on_cos[:, branches:] - on_sin[:, :branches]
    return (out_real * out_real + out_imag * out_imag) / frames


def solution(mesh):
    in_specs = (P("cell", "tm", None), P("cell", None), P(), P(("tm", "cell"), None, None, None))
    out_specs = P(("tm", "cell"), None, None)
    return jax.shard_map(local, mesh=mesh, in_specs=in_specs, out_specs=out_specs, check_vma=False)
```

profile of v0, /device:TPU:1, one launch (start us, length us, event | category | flops | bytes accessed | tf_op | source)
XLA Modules:
  0.0 152.7 jit_solution(2938117541314478069)
XLA Ops:
  0.0 7.5 %all-to-all-start = ((bf16[512,8,192]{0,2,1:T(8,128)(2,1)}), bf16[512,8,192]{0,2,1:T(8,128)(2,1)S(1)}, u32[]{:S(2)}, u32[]{:S(2)}) async-start(bf16[512,8,192]{0,2,1:T(8,128)(2,1)} %bitcast.57), calls=%async_computation | async-start | bytes 3145728 | tf_op jit(solution)/shard_map/all_to_all | solution.py:63
  7.6 0.6 fusion.34
  8.2 0.7 fusion.33
  8.9 42.0 %all_gather.3 = s32[4096,3]{0,1:T(4,128)S(1)} all-gather(s32[512,3]{0,1:T(4,128)} %param.5), channel_id=1, replica_groups=mesh['tm'=32,'cell'=8] {'cell'}, dimensions={0}, use_global_device_ids=true | all-gather | bytes 55296 | tf_op jit(solution)/shard_map/all_gather | solution.py:65
  50.9 0.8 fusion.32
  51.7 13.9 %negate_select_fusion.1 = (bf16[512,1,4096]{2,0,1:T(8,128)(2,1)S(1)}, bf16[512,1,4096]{2,0,1:T(8,128)(2,1)}) fusion(bf16[]{:T(256)} %bitcast.13, bf16[]{:T(256)} %bitcast.12, bf16[]{:T(256)} %bitcast.11, bf16[]{:T(256)} %bitcast.10, bf16[]{:T(256)} %bitcast.9, bf16[]{:T(256)} %bitcast.8, bf16[]{:T(256)} %bitcast.7, bf16[]{:T(256)} %bitcast.6, ...), kind=kLoop, calls=%fused_computation.7 | loop fusion | flops 67108864 | bytes 8443920 | tf_op jit(solution)/shard_map/jit(_where)/select_n | solution.py:34
  65.6 6.2 %pad_maximum_fusion = bf16[512,2,4096]{2,0,1:T(8,128)(2,1)} fusion(bf16[512,1,4096]{2,0,1:T(8,128)(2,1)} %get-tuple-element.15, bf16[512,1,4096]{2,0,1:T(8,128)(2,1)S(1)} %get-tuple-element.14), kind=kLoop, calls=%fused_computation | loop fusion | flops 4194304 | bytes 16777216 | tf_op jit(solution)/shard_map/stack | solution.py:35
  71.7 16.4 %copy.35 = bf16[512,2,4096]{2,1,0:T(2,128)(2,1)} copy(bf16[512,2,4096]{2,0,1:T(8,128)(2,1)} %pad_maximum_fusion) | data formatting | bytes 16777216 | tf_op jit(solution)/shard_map/stack | solution.py:35
  88.1 0.0 copy-start
  88.1 13.2 %reshape.499 = bf16[1024,4096]{1,0:T(8,128)(2,1)} reshape(bf16[512,2,4096]{2,1,0:T(2,128)(2,1)} %copy.35) | data formatting | bytes 16777216 | tf_op jit(solution)/shard_map/reshape | solution.py:66
  101.3 0.0 copy-done
  101.3 0.1 copy.48
  101.4 0.0 all-to-all-done
  101.5 0.2 copy.49
  101.6 6.3 %convolution_convert_fusion = bf16[1024,192]{0,1:T(8,128)(2,1)S(1)} fusion(bf16[1024,4096]{1,0:T(8,128)(2,1)} %reshape.499, bf16[4096,192]{0,1:T(8,128)(2,1)S(1)} %bitcast.58), kind=kOutput, calls=%fused_computation.15 | convolution fusion | flops 1610809344 | bytes 10354688 | tf_op jit(solution)/shard_map/dot_general | solution.py:67
  108.0 0.2 copy.37
  108.2 0.3 reshape.502
  108.5 1.2 copy.38
  109.6 16.1 %all-to-all-start.1 = ((bf16[256,2,2,2,96]{4,2,3,1,0:T(2,128)(2,1)}), bf16[256,2,2,2,96]{4,2,3,1,0:T(2,128)(2,1)S(1)}, u32[]{:S(2)}, u32[]{:S(2)}) async-start(bf16[256,2,2,2,96]{4,2,3,1,0:T(2,128)(2,1)} %copy.38), calls=%async_computation.1 | async-start | bytes 1048576 | tf_op jit(solution)/shard_map/all_to_all | solution.py:69
  125.8 0.1 fusion.25
  125.9 0.1 copy.47
  126.0 0.3 fusion.22
  126.4 0.3 multiply_subtract_fusion
  126.7 19.2 %all-to-all-done.1 = bf16[256,2,2,2,96]{4,2,3,1,0:T(2,128)(2,1)S(1)} async-done(((bf16[256,2,2,2,96]{4,2,3,1,0:T(2,128)(2,1)}), bf16[256,2,2,2,96]{4,2,3,1,0:T(2,128)(2,1)S(1)}, u32[]{:S(2)}, u32[]{:S(2)}) %all-to-all-start.1) | async-done | bytes 393248 | tf_op jit(solution)/shard_map/all_to_all | solution.py:69
  145.9 1.6 %convolution_bitcast_fusion = f32[2,256,2,192]{1,3,2,0:T(8,128)} fusion(bf16[256,2,2,2,96]{4,2,3,1,0:T(2,128)(2,1)S(1)} %all-to-all-done.1, f32[2,1,96,192]{2,3,1,0:T(8,128)S(1)} %get-tuple-element.10, f32[2,1,96,192]{2,3,1,0:T(8,128)S(1)} %get-tuple-element.9), kind=kOutput, calls=%fused_computation.14 | convolution fusion | flops 453058560 | bytes 1474560 | tf_op jit(solution)/shard_map/sjrfk,jrkc->jsfc/dot_general | solution.py:78
  147.5 1.5 %copy.43 = f32[2,256,2,192]{3,0,2,1:T(2,128)S(1)} copy(f32[2,256,2,192]{1,3,2,0:T(8,128)} %convolution_bitcast_fusion) | data formatting | bytes 1572864 | tf_op jit(solution)/shard_map/sjrfk,jrkc->jsfc/dot_general | solution.py:78
  149.0 2.7 %fusion = f32[2,192,1024]{2,1,0:T(8,128)S(1)} fusion(f32[512,512]{1,0:T(8,128)S(1)} %bitcast.56, f32[512,512]{1,0:T(8,128)S(1)} %bitcast.55, f32[2,512,192]{2,0,1:T(2,128)S(1)} %bitcast.54), kind=kOutput, calls=%fused_computation.11 | convolution fusion | flops 2416443392 | bytes 4456448 | tf_op jit(solution)/shard_map/jts,tw->jsw/dot_general | solution.py:83
  151.8 0.9 fusion.7
  (7 shorter events, 0.2 us)
Async XLA Ops:
  0.0 101.4 %all-to-all-start = ((bf16[512,8,192]{0,2,1:T(8,128)(2,1)}), bf16[512,8,192]{0,2,1:T(8,128)(2,1)S(1)}, u32[]{:S(2)}, u32[]{:S(2)}) async-start(bf16[512,8,192]{0,2,1:T(8,128)(2,1)} %bitcast.57), calls=%async_computation | async-start | bytes 3145728 | tf_op jit(solution)/shard_map/all_to_all | solution.py:63
  88.1 13.2 %copy-start = (f32[2,2,96,96]{3,2,1,0:T(8,128)S(1)}, f32[2,2,96,96]{3,2,1,0:T(8,128)}, u32[]{:S(2)}) copy-start(f32[2,2,96,96]{3,2,1,0:T(8,128)} %param.7) | copy-start | bytes 442372
  109.6 36.3 %all-to-all-start.1 = ((bf16[256,2,2,2,96]{4,2,3,1,0:T(2,128)(2,1)}), bf16[256,2,2,2,96]{4,2,3,1,0:T(2,128)(2,1)S(1)}, u32[]{:S(2)}, u32[]{:S(2)}) async-start(bf16[256,2,2,2,96]{4,2,3,1,0:T(2,128)(2,1)} %copy.38), calls=%async_computation.1 | async-start | bytes 1048576 | tf_op jit(solution)/shard_map/all_to_all | solution.py:69
where the time goes:
time: 153 us
  blocking collectives  42 us (27%)
  local copies, waits for them, and re-layouts  35.2 us (23%)
  starting transfers between devices  23.6 us (15%)
  other arithmetic  21.8 us (14%)
  waiting for transfers between devices  19.2 us (13%)
  matrix products  10.7 us (7%)
    all_gather x1, blocking collectives, local(): all_coords = lax.all_gather(cell_coords, 'cell', axis=0, tiled=True)  42 us
    all_to_all x1, waiting for transfers between devices, local(): lax.all_to_all(modes, ('tm', 'cell'), split_axis=0, concat_axis=0, tiled=...  19.2 us
    another operation x1, local copies, waits for them, and re-layouts, phase_rows(): return jnp.stack([real, imag], axis=1)  16.4 us
    all_to_all x1, starting transfers between devices, local(): lax.all_to_all(modes, ('tm', 'cell'), split_axis=0, concat_axis=0, tiled=...  16.1 us
    select_n x1, other arithmetic, phase_rows(): real, imag = (jnp.where(bit3, -real, real), jnp.where(bit3, -imag, imag))  13.9 us
    reshape x1, local copies, waits for them, and re-layouts, local(): phase_rows(q_coords, all_coords).reshape(2 * q_total, cell_dev * n_cell)  13.2 us
    all_to_all x1, starting transfers between devices, local(): lax.all_to_all(spread, 'cell', split_axis=1, concat_axis=0, tiled=True)  7.48 us
    dot_general x1, matrix products, local(): modes = jnp.dot(table, all_cells, preferred_element_type=jnp.float32)  6.34 us
  transfers between devices with their start and end apart: 2, of which 1 were waited for; matrix products, arithmetic and copies ran while one was open for 35% of the time, Pallas kernels for 0%

commit v1 on v0

--- a/solution.py
+++ b/solution.py
@@ -62,7 +62,9 @@
     spread = velocity.reshape(cell_dev, n_cell, frames_each * branches)
     all_cells = lax.all_to_all(spread, "cell", split_axis=1, concat_axis=0, tiled=True)
     all_cells = all_cells.reshape(cell_dev * n_cell, frames_each * branches)
-    all_coords = lax.all_gather(cell_coords, "cell", axis=0, tiled=True)
+    all_coords = jnp.concatenate(
+        lax.all_to_all(jnp.stack([cell_coords] * lax.axis_size("cell")), "cell", 0, 0), axis=0
+    )
     table = phase_rows(q_coords, all_coords).reshape(2 * q_total, cell_dev * n_cell)
     modes = jnp.dot(table, all_cells, preferred_element_type=jnp.float32)
     modes = modes.astype(jnp.bfloat16).reshape(n_dev, q_local, 2, frames_each, branches)

time: 153 us -> 121 us (0.79)
  blocking collectives: 42 us -> 0 us
  starting transfers between devices: 23.6 us -> 27.5 us
  waiting for transfers between devices: 19.2 us -> 22.6 us
  local copies, waits for them, and re-layouts: 35.2 us -> 37.5 us
    all_gather x1 -> x0, blocking collectives: 42 us -> none  [local(): all_coords = lax.all_gather(cell_coords, 'cell', axis=0, tiled=True)]
    all_to_all x0 -> x1, starting transfers between devices: none -> 7.48 us  [local(): lax.all_to_all(jnp.stack([cell_coords] * lax.axis_size('cell')), 'cell',...]
    all_to_all x1, starting transfers between devices: 7.48 us -> 3.58 us  [local(): lax.all_to_all(spread, 'cell', split_axis=1, concat_axis=0, tiled=True)]
    all_to_all x0 -> x1, waiting for transfers between devices: none -> 3.39 us  [local(): lax.all_to_all(jnp.stack([cell_coords] * lax.axis_size('cell')), 'cell',...]
  transfers between devices with their start and end apart: 2 -> 3, of which waited for: 1 -> 2; matrix products, arithmetic and copies ran while one was open for 35% -> 45% of each run, Pallas kernels for 0% -> 0%
where the time goes in v1:
time: 121 us; the launch traced here: 120 us
  local copies, waits for them, and re-layouts  37.5 us (31%)
  starting transfers between devices  27.5 us (23%)
  waiting for transfers between devices  22.6 us (19%)
  other arithmetic  21.8 us (18%)
  matrix products  10.7 us (9%)
    all_to_all x1, waiting for transfers between devices, local(): lax.all_to_all(modes, ('tm', 'cell'), split_axis=0, concat_axis=0, tiled=...  19.2 us
    all_to_all x1, starting transfers between devices, local(): lax.all_to_all(modes, ('tm', 'cell'), split_axis=0, concat_axis=0, tiled=...  16.5 us
    another operation x1, local copies, waits for them, and re-layouts, phase_rows(): return jnp.stack([real, imag], axis=1)  16.4 us
    select_n x1, other arithmetic, phase_rows(): real, imag = (jnp.where(bit3, -real, real), jnp.where(bit3, -imag, imag))  13.9 us
    reshape x1, local copies, waits for them, and re-layouts, local(): phase_rows(q_coords, all_coords).reshape(2 * q_total, cell_dev * n_cell)  13.1 us
    all_to_all x1, starting transfers between devices, local(): lax.all_to_all(jnp.stack([cell_coords] * lax.axis_size('cell')), 'cell',...  7.48 us
    dot_general x1, matrix products, local(): modes = jnp.dot(table, all_cells, preferred_element_type=jnp.float32)  6.33 us
    another operation x1, other arithmetic, phase_rows(): return jnp.stack([real, imag], axis=1)  6.18 us
  transfers between devices with their start and end apart: 3, of which 2 were waited for; matrix products, arithmetic and copies ran while one was open for 45% of the time, Pallas kernels for 0%

profile of v1, /device:TPU:1, one launch (start us, length us, event | category | flops | bytes accessed | tf_op | source)
XLA Modules:
  0.0 120.3 jit_solution(16276872743622371757)
XLA Ops:
  0.0 1.3 %stack.10 = s32[8,512,3]{1,2,0:T(4,128)} broadcast(s32[512,3]{0,1:T(4,128)} %param.5), dimensions={1,2} | broadcast | bytes 55296 | tf_op jit(solution)/shard_map/stack | solution.py:66
  1.3 7.5 %all-to-all-start = ((s32[8,512,3]{1,2,0:T(4,128)}), s32[8,512,3]{1,2,0:T(4,128)S(1)}, u32[]{:S(2)}, u32[]{:S(2)}) async-start(s32[8,512,3]{1,2,0:T(4,128)} %stack.10), calls=%async_computation | async-start | bytes 131072 | tf_op jit(solution)/shard_map/all_to_all | solution.py:66
  8.9 0.7 fusion.33
  9.6 0.8 fusion.32
  10.4 1.0 fusion.30
  11.3 0.1 copy.49
  11.5 0.7 fusion.34
  12.1 3.4 %all-to-all-done = s32[8,512,3]{1,2,0:T(4,128)S(1)} async-done(((s32[8,512,3]{1,2,0:T(4,128)}), s32[8,512,3]{1,2,0:T(4,128)S(1)}, u32[]{:S(2)}, u32[]{:S(2)}) %all-to-all-start) | async-done | bytes 49184 | tf_op jit(solution)/shard_map/all_to_all | solution.py:66
  15.5 3.6 %all-to-all-start.1 = ((bf16[512,8,192]{0,2,1:T(8,128)(2,1)}), bf16[512,8,192]{0,2,1:T(8,128)(2,1)S(1)}, u32[]{:S(2)}, u32[]{:S(2)}) async-start(bf16[512,8,192]{0,2,1:T(8,128)(2,1)} %bitcast.58), calls=%async_computation.1 | async-start | bytes 3145728 | tf_op jit(solution)/shard_map/all_to_all | solution.py:63
  19.2 13.9 %negate_select_fusion.1 = (bf16[512,1,4096]{2,0,1:T(8,128)(2,1)S(1)}, bf16[512,1,4096]{2,0,1:T(8,128)(2,1)}) fusion(bf16[]{:T(256)} %bitcast.14, bf16[]{:T(256)} %bitcast.13, bf16[]{:T(256)} %bitcast.12, bf16[]{:T(256)} %bitcast.11, bf16[]{:T(256)} %bitcast.10, bf16[]{:T(256)} %bitcast.9, bf16[]{:T(256)} %bitcast.8, bf16[]{:T(256)} %bitcast.7, ...), kind=kLoop, calls=%fused_computation.7 | loop fusion | flops 67108864 | bytes 8443920 | tf_op jit(solution)/shard_map/jit(_where)/select_n | solution.py:34
  33.0 6.2 %pad_maximum_fusion = bf16[512,2,4096]{2,0,1:T(8,128)(2,1)} fusion(bf16[512,1,4096]{2,0,1:T(8,128)(2,1)} %get-tuple-element.15, bf16[512,1,4096]{2,0,1:T(8,128)(2,1)S(1)} %get-tuple-element.14), kind=kLoop, calls=%fused_computation | loop fusion | flops 4194304 | bytes 16777216 | tf_op jit(solution)/shard_map/stack | solution.py:35
  39.2 16.4 %copy.36 = bf16[512,2,4096]{2,1,0:T(2,128)(2,1)} copy(bf16[512,2,4096]{2,0,1:T(8,128)(2,1)} %pad_maximum_fusion) | data formatting | bytes 16777216 | tf_op jit(solution)/shard_map/stack | solution.py:35
  55.6 13.1 %reshape.505 = bf16[1024,4096]{1,0:T(8,128)(2,1)} reshape(bf16[512,2,4096]{2,1,0:T(2,128)(2,1)} %copy.36) | data formatting | bytes 16777216 | tf_op jit(solution)/shard_map/reshape | solution.py:68
  68.8 0.0 all-to-all-done.1
  68.8 0.2 copy.50
  68.9 6.3 %convolution_convert_fusion = bf16[1024,192]{0,1:T(8,128)(2,1)S(1)} fusion(bf16[1024,4096]{1,0:T(8,128)(2,1)} %reshape.505, bf16[4096,192]{0,1:T(8,128)(2,1)S(1)} %bitcast.59), kind=kOutput, calls=%fused_computation.15 | convolution fusion | flops 1610809344 | bytes 10354688 | tf_op jit(solution)/shard_map/dot_general | solution.py:69
  75.3 0.2 copy.38
  75.5 0.3 reshape.508
  75.8 1.2 copy.39
  76.9 16.5 %all-to-all-start.2 = ((bf16[256,2,2,2,96]{4,2,3,1,0:T(2,128)(2,1)}), bf16[256,2,2,2,96]{4,2,3,1,0:T(2,128)(2,1)S(1)}, u32[]{:S(2)}, u32[]{:S(2)}) async-start(bf16[256,2,2,2,96]{4,2,3,1,0:T(2,128)(2,1)} %copy.39), calls=%async_computation.2 | async-start | bytes 1048576 | tf_op jit(solution)/shard_map/all_to_all | solution.py:71
  93.4 0.1 fusion.25
  93.5 0.1 copy.48
  93.6 0.3 fusion.22
  94.0 0.3 multiply_subtract_fusion
  94.3 19.2 %all-to-all-done.2 = bf16[256,2,2,2,96]{4,2,3,1,0:T(2,128)(2,1)S(1)} async-done(((bf16[256,2,2,2,96]{4,2,3,1,0:T(2,128)(2,1)}), bf16[256,2,2,2,96]{4,2,3,1,0:T(2,128)(2,1)S(1)}, u32[]{:S(2)}, u32[]{:S(2)}) %all-to-all-start.2) | async-done | bytes 393248 | tf_op jit(solution)/shard_map/all_to_all | solution.py:71
  113.5 1.6 %convolution_bitcast_fusion = f32[2,256,2,192]{1,3,2,0:T(8,128)} fusion(bf16[256,2,2,2,96]{4,2,3,1,0:T(2,128)(2,1)S(1)} %all-to-all-done.2, f32[2,1,96,192]{2,3,1,0:T(8,128)S(1)} %get-tuple-element.10, f32[2,1,96,192]{2,3,1,0:T(8,128)S(1)} %get-tuple-element.9), kind=kOutput, calls=%fused_computation.14 | convolution fusion | flops 453058560 | bytes 1474560 | tf_op jit(solution)/shard_map/sjrfk,jrkc->jsfc/dot_general | solution.py:80
  115.1 1.5 %copy.44 = f32[2,256,2,192]{3,0,2,1:T(2,128)S(1)} copy(f32[2,256,2,192]{1,3,2,0:T(8,128)} %convolution_bitcast_fusion) | data formatting | bytes 1572864 | tf_op jit(solution)/shard_map/sjrfk,jrkc->jsfc/dot_general | solution.py:80
  116.6 2.7 %fusion = f32[2,192,1024]{2,1,0:T(8,128)S(1)} fusion(f32[512,512]{1,0:T(8,128)S(1)} %bitcast.57, f32[512,512]{1,0:T(8,128)S(1)} %bitcast.56, f32[2,512,192]{2,0,1:T(2,128)S(1)} %bitcast.55), kind=kOutput, calls=%fused_computation.11 | convolution fusion | flops 2416443392 | bytes 4456448 | tf_op jit(solution)/shard_map/jts,tw->jsw/dot_general | solution.py:85
  119.4 0.9 fusion.7
  (6 shorter events, 0.2 us)
Async XLA Ops:
  1.3 14.2 %all-to-all-start = ((s32[8,512,3]{1,2,0:T(4,128)}), s32[8,512,3]{1,2,0:T(4,128)S(1)}, u32[]{:S(2)}, u32[]{:S(2)}) async-start(s32[8,512,3]{1,2,0:T(4,128)} %stack.10), calls=%async_computation | async-start | bytes 131072 | tf_op jit(solution)/shard_map/all_to_all | solution.py:66
  15.5 53.2 %all-to-all-start.1 = ((bf16[512,8,192]{0,2,1:T(8,128)(2,1)}), bf16[512,8,192]{0,2,1:T(8,128)(2,1)S(1)}, u32[]{:S(2)}, u32[]{:S(2)}) async-start(bf16[512,8,192]{0,2,1:T(8,128)(2,1)} %bitcast.58), calls=%async_computation.1 | async-start | bytes 3145728 | tf_op jit(solution)/shard_map/all_to_all | solution.py:63
  76.9 36.6 %all-to-all-start.2 = ((bf16[256,2,2,2,96]{4,2,3,1,0:T(2,128)(2,1)}), bf16[256,2,2,2,96]{4,2,3,1,0:T(2,128)(2,1)S(1)}, u32[]{:S(2)}, u32[]{:S(2)}) async-start(bf16[256,2,2,2,96]{4,2,3,1,0:T(2,128)(2,1)} %copy.39), calls=%async_computation.2 | async-start | bytes 1048576 | tf_op jit(solution)/shard_map/all_to_all | solution.py:71
